TPU v7x, 32 devices: a whole 2x2x4 slice. The times are simulated.
32 devices in a mesh: clu: 8 (over z, y), sub: 4 (over x, core).
Axes of the slice: x: 2, y: 2, z: 4, core: 2. Of those that a mesh axis runs over, the one named last changes fastest.
Arguments:
- queries: bfloat16 [32768, 768], P(('clu', 'sub')), may hold values from -6 to 6
- pos_cols: int32 [6, 32768], P(None, 'clu'), may hold values from 0 to 1023, as said below
- label_ids: int32 [8192], P(('clu', 'sub')), may hold values from 0 to 65535, as said below
- slot_of: int32 [65536], replicated, may hold values from 0 to 65535, as said below
- label_table: bfloat16 [768, 65536], P('sub', 'clu'), may hold values from -5 to 5
- label_freq: int32 [65536], P('clu'), may hold values from 1 to 65535
- first_moment: float32 [768, 65536], P('sub', 'clu'), may hold values from -3 to 3
- second_moment: float32 [768, 65536], P('sub', 'clu'), may hold values from 0.05 to 1
Outputs:
- new_table: bfloat16 [768, 65536], P('sub', 'clu')
- new_first: float32 [768, 65536], P('sub', 'clu')
- new_second: float32 [768, 65536], P('sub', 'clu')
- mean_loss: float32 [], replicated
Inputs may be any that keep to these rules, and one draw needn't show every extreme that they name: `label_ids`: the 256 ids of one device's list are distinct. Among them at most 96 have slot_of[id] // 8192 equal to one value; in every draw one such value is reached by exactly 96 ids of every list. `pos_cols`: each query names 1 to 6 distinct columns of its batch's 4 * 256 columns; entries of a query may repeat. `slot_of`: A permutation of the label slots.
All inputs are finite; a program needn't handle non-finite values.
Results may differ from a plain program's by a relative error of at most 0.0023.
Values may be sent and summed in bfloat16 or wider, within the bound.
No kernel may reach another device: no remote copies, remote signals or barrier semaphores. Data moves between devices by JAX's collectives and lax.ppermute only.
A program may use at most 128 MiB of HBM per device.

v0:
```python
import math

import jax
import jax.numpy as jnp
from jax import lax
from jax.sharding import PartitionSpec as P

LOSS_SCALE = 1048576


FOCUS_ALPHA = 0.25
BETA_FIRST = 0.9
BETA_SECOND = 0.999
LEARN_RATE = 0.01
EPSILON = 1e-08


def focal_terms(logits, target, weight):
    probability = jax.nn.sigmoid(logits)
    complement = 1.0 - probability
    soft_neg = jax.nn.softplus(-logits)
    soft_pos = jax.nn.softplus(logits)
    weight_row = weight[None, :]
    losses = weight_row * (
        target * FOCUS_ALPHA * complement * complement * soft_neg
        + (1.0 - target) * (1.0 - FOCUS_ALPHA) * probability * probability * soft_pos
    )
    slopes = weight_row * (
        target
        * -FOCUS_ALPHA
        * complement
        * complement
        * (2.0 * probability * soft_neg + complement)
        + (1.0 - target)
        * (1.0 - FOCUS_ALPHA)
        * probability
        * probability
        * (2.0 * complement * soft_pos + probability)
    )
    return (losses, slopes.astype(jnp.bfloat16))


def positive_mask(listed, columns):
    found = jnp.zeros((listed.shape[1], columns.shape[0]), jnp.float32)
    for k in range(listed.shape[0]):
        found = jnp.maximum(found, (listed[k][:, None] == columns[None, :]).astype(jnp.float32))
    return found


def body(
    queries, pos_cols, label_ids, slot_of, label_table, label_freq, first_moment, second_moment
):
    clu_count = lax.axis_size("clu")
    sub_count = lax.axis_size("sub")
    my_sub = lax.axis_index("sub")
    list_len = label_ids.shape[0]
    col_width = label_table.shape[0]
    lab_rows = label_table.shape[1]
    width = col_width * sub_count
    slot_cap = 3 * list_len // clu_count
    inv_root = 1.0 / math.sqrt(width)
    slot_ids = slot_of[label_ids]
    owner_of = slot_ids // lab_rows
    local_row = slot_ids % lab_rows
    one_hot = (owner_of[:, None] == jnp.arange(clu_count, dtype=jnp.int32)[None, :]).astype(
        jnp.int32
    )
    slot_rank = jnp.sum(jnp.cumsum(one_hot, axis=0) * one_hot, axis=1) - 1
    requests = (
        jnp.full((clu_count, slot_cap), lab_rows, jnp.int32).at[owner_of, slot_rank].set(local_row)
    )
    columns = my_sub * list_len + jnp.arange(list_len, dtype=jnp.int32)
    lower = my_sub * list_len
    fresh_total = jnp.zeros((), jnp.float32)
    for k in range(pos_cols.shape[0]):
        fresh = jnp.logical_and(pos_cols[k] >= lower, pos_cols[k] < lower + list_len)
        for j in range(k):
            fresh = jnp.logical_and(fresh, pos_cols[j] != pos_cols[k])
        fresh_total = fresh_total + jnp.sum(fresh.astype(jnp.float32))
    positives = lax.psum(fresh_total, ("clu", "sub"))
    factor = LOSS_SCALE / (math.sqrt(width) * positives)
    wanted = jnp.broadcast_to(requests[:, None, :], (clu_count, sub_count, slot_cap)).reshape(
        clu_count * sub_count, slot_cap
    )
    asked = lax.all_to_all(wanted, ("clu", "sub"), split_axis=0, concat_axis=0, tiled=True)
    picked = jnp.clip(asked, 0, lab_rows - 1)
    got_rows, got_freq = (
        lax.all_to_all(
            label_table[:, picked], ("clu", "sub"), split_axis=1, concat_axis=1, tiled=True
        ),
        lax.all_to_all(
            label_freq[picked][None], ("clu", "sub"), split_axis=1, concat_axis=1, tiled=True
        ),
    )
    arranged = got_rows.reshape(col_width, clu_count, sub_count, slot_cap)
    full_cols = jnp.transpose(arranged[:, owner_of, :, slot_rank], (2, 1, 0)).reshape(
        width, list_len
    )
    fetched_freq = got_freq.reshape(clu_count, sub_count, slot_cap)[owner_of, 0, slot_rank]
    owner_requests = asked.reshape(-1)
    weights = 1.0 / (1.0 + jnp.log1p(fetched_freq.astype(jnp.float32)))
    initial = (jnp.zeros((width, list_len), jnp.float32), jnp.zeros((), jnp.float32))
    arrived = lax.all_gather(queries, "sub", axis=0, tiled=True)
    count_rows = arrived.shape[0]
    block = 512

    def one_block(step, partial_value):
        q_block = lax.dynamic_slice_in_dim(arrived, step * block, block, 0)
        p_block = lax.dynamic_slice_in_dim(pos_cols, step * block, block, 1)
        target = positive_mask(p_block, columns)
        logits = (
            lax.dot_general(
                q_block, full_cols, (((1,), (0,)), ((), ())), preferred_element_type=jnp.float32
            )
            * inv_root
        )
        losses, slopes = focal_terms(logits, target, weights)
        gradient = partial_value[0] + lax.dot_general(
            q_block, slopes, (((0,), (0,)), ((), ())), preferred_element_type=jnp.float32
        )
        return (gradient, partial_value[1] + jnp.sum(losses))

    gradient, loss_here = lax.fori_loop(0, count_rows // block, one_block, initial)
    loss_sum = lax.psum(loss_here, ("clu", "sub"))
    outgoing = gradient * factor
    pieces = jnp.transpose(outgoing.reshape(sub_count, col_width, list_len), (2, 1, 0))
    buffer = (
        jnp.zeros((col_width, clu_count, sub_count, slot_cap), jnp.float32)
        .at[:, owner_of, :, slot_rank]
        .set(pieces)
    )
    received = lax.all_to_all(
        buffer.reshape(col_width, clu_count * sub_count, slot_cap),
        ("clu", "sub"),
        split_axis=1,
        concat_axis=1,
        tiled=True,
    )
    summed = (
        jnp.zeros((col_width, lab_rows + 1), jnp.float32)
        .at[:, owner_requests]
        .add(received.reshape(col_width, -1))[:, :lab_rows]
    )
    marks = jax.ops.segment_sum(
        jnp.ones(owner_requests.shape, jnp.float32), owner_requests, num_segments=lab_rows + 1
    )[:lab_rows]
    hits = (marks > 0.5)[None, :]
    new_first = jnp.where(
        hits, BETA_FIRST * first_moment + (1.0 - BETA_FIRST) * summed, first_moment
    )
    new_second = jnp.where(
        hits, BETA_SECOND * second_moment + (1.0 - BETA_SECOND) * summed * summed, second_moment
    )
    base_table = label_table.astype(jnp.float32)
    moved = base_table - LEARN_RATE * new_first / (jnp.sqrt(new_second) + EPSILON)
    new_table = jnp.where(hits, moved, base_table).astype(jnp.bfloat16)
    mean_loss = loss_sum / positives
    return (new_table, new_first, new_second, mean_loss)


def solution(mesh):
    in_specs = (
        P(("clu", "sub"), None),
        P(None, "clu"),
        P(("clu", "sub")),
        P(),
        P("sub", "clu"),
        P("clu"),
        P("sub", "clu"),
        P("sub", "clu"),
    )
    out_specs = (P("sub", "clu"), P("sub", "clu"), P("sub", "clu"), P())
    return jax.shard_map(body, mesh=mesh, in_specs=in_specs, out_specs=out_specs, check_vma=False)
```

profile of v0, /device:TPU:0, one launch (start us, length us, event | category | flops | bytes accessed | tf_op | source)
XLA Modules:
  0.0 400.0 jit_solution(17738478672535067182)
XLA Ops:
  11.4 11.1 %scatter_fusion = s32[8,96]{1,0:T(8,128)S(1)} fusion(s32[8,96]{1,0:T(8,128)S(1)} %broadcast_in_dim.78, s32[256]{0:T(256)S(1)} %bitcast.61, s32[256]{0:T(256)S(1)} %get-tuple-element.241), kind=kCustom, calls=%fused_computation.5 | custom fusion | bytes 5120 | tf_op jit(solution)/shard_map/scatter | solution.py:70
  22.5 14.3 %all_to_all.24 = s32[32,1,96]{2,1,0:T(1,128)S(1)} all-to-all(s32[32,1,96]{2,1,0:T(1,128)S(1)} %bitcast.74), channel_id=1, replica_groups=mesh['clu'=8,'sub'=4] {'clu','sub'}, dimensions={0} | all-to-all | bytes 24576 | tf_op jit(solution)/shard_map/all_to_all | solution.py:85
  38.1 17.4 %gather_fusion.1 = s32[3072]{0:T(1024)S(1)} fusion(s32[8192]{0:T(1024)S(1)} %copy-done.2, s32[3072]{0:T(1024)S(1)} %broadcast_clamp_fusion.1), kind=kCustom, calls=%fused_computation.1 | custom fusion | bytes 36864 | tf_op jit(solution)/shard_map/gather | solution.py:92
  58.8 3.9 copy.50
  62.7 12.6 %gather_fusion.3 = bf16[3072,192]{1,0:T(8,128)(2,1)S(1)} fusion(bf16[192,8192]{0,1:T(8,128)(2,1)} %copy.50, s32[3072]{0:T(1024)S(1)} %broadcast_clamp_fusion.1), kind=kCustom, calls=%fused_computation.3 | custom fusion | bytes 2371584 | tf_op jit(solution)/shard_map/gather | solution.py:89
  76.9 5.8 %all-to-all-start.2 = ((bf16[192,32,96]{2,0,1:T(8,128)(2,1)}), bf16[192,32,96]{2,0,1:T(8,128)(2,1)S(1)}, u32[]{:S(2)}, u32[]{:S(2)}) async-start(bf16[192,32,96]{2,0,1:T(8,128)(2,1)} %bitcast.13), calls=%async_computation.2 | async-start | bytes 3145728 | tf_op jit(solution)/shard_map/all_to_all | solution.py:88
  90.1 30.4 %all-to-all-done.2 = bf16[192,32,96]{2,0,1:T(8,128)(2,1)S(1)} async-done(((bf16[192,32,96]{2,0,1:T(8,128)(2,1)}), bf16[192,32,96]{2,0,1:T(8,128)(2,1)S(1)}, u32[]{:S(2)}, u32[]{:S(2)}) %all-to-all-start.2) | async-done | bytes 1179680 | tf_op jit(solution)/shard_map/all_to_all | solution.py:88
  123.6 56.4 %while.16 = (s32[]{:T(128)}, f32[768,256]{1,0:T(8,128)S(1)}, f32[]{:T(128)}, bf16[4096,768]{1,0:T(8,128)(2,1)}, f32[256]{0:T(256)S(1)}, /*index=5*/s32[6,4096]{1...) while((s32[]{:T(128)}, f32[768,256]{1,0:T(8,128)S(1)}, ...), condition=%wide.region_7.8_spmd.clone, body=%wide.region_5.7_spmd.clone.sunk | while | flops 416022784 | bytes 4642125 | solution.py:123
  144.9 3.2 fusion.57
  166.0 3.2 fusion.57
  180.0 38.8 %all-reduce = (f32[]{:T(128)}, f32[]{:T(128)}) all-reduce(f32[]{:T(128)S(6)} %add.248, f32[]{:T(128)} %get-tuple-element.145), channel_id=1, replica_groups=mesh['clu'=8,'sub'=4] {'clu','sub'}, use_global_device_ids=true, to_apply=%region_14.15 | all-reduce | flops 2 | bytes 16 | tf_op jit(solution)/shard_map/psum | solution.py:80
  221.3 16.8 %scatter_fusion.1 = f32[192,8,4,96]{0,2,3,1:T(4,128)S(1)} fusion(f32[192,8,4,96]{0,2,3,1:T(4,128)S(1)} %broadcast_in_dim.84, s32[256]{0:T(256)S(1)} %bitcast.62, f32[256,192,4]{1,2,0:T(4,128)} %bitcast.69), kind=kCustom, calls=%fused_computation.7 | custom fusion | bytes 2361344 | tf_op jit(solution)/shard_map/scatter | solution.py:130
  241.0 5.2 %all-to-all-start.3 = ((f32[192,32,96]{2,0,1:T(8,128)}), f32[192,32,96]{2,0,1:T(8,128)S(1)}, u32[]{:S(2)}, u32[]{:S(2)}) async-start(f32[192,32,96]{2,0,1:T(8,128)} %bitcast.65), calls=%async_computation.3 | async-start | bytes 6291456 | tf_op jit(solution)/shard_map/all_to_all | solution.py:132
  246.2 8.4 %copy.51 = f32[192,8192]{0,1:T(8,128)} copy(f32[192,8192]{1,0:T(8,128)} %param.16) | data formatting | bytes 12582912 | tf_op args[6]
  254.7 8.5 %copy.61 = f32[192,8192]{0,1:T(8,128)} copy(f32[192,8192]{1,0:T(8,128)} %param.17) | data formatting | bytes 12582912 | tf_op args[7]
  263.3 20.7 %scatter_custom_fusion.1 = f32[8193]{0:T(1024)S(1)} fusion(s32[3072]{0:T(1024)S(1)} %reshape.307, f32[3072]{0:T(1024)S(1)} %broadcast.344, f32[]{:T(128)} %constant.135.clone.1), kind=kCustom, calls=%fused_computation.70 | custom fusion | flops 3072 | bytes 32776 | tf_op jit(solution)/shard_map/scatter-add | solution.py:144
  285.4 32.3 %all-to-all-done.3 = f32[192,32,96]{2,0,1:T(8,128)S(1)} async-done(((f32[192,32,96]{2,0,1:T(8,128)}), f32[192,32,96]{2,0,1:T(8,128)S(1)}, u32[]{:S(2)}, u32[]{:S(2)}) %all-to-all-start.3) | async-done | bytes 2359328 | tf_op jit(solution)/shard_map/all_to_all | solution.py:132
  317.7 3.5 copy.58
  321.2 3.4 reshape.320
  326.9 24.0 %scatter_custom_fusion.3 = f32[192,8193]{0,1:T(8,128)} fusion(s32[3072]{0:T(1024)S(1)} %bitcast.88, f32[3072,192]{1,0:T(8,128)} %copy.59, f32[]{:T(128)} %constant.135.clone.1), kind=kCustom, calls=%fused_computation.58 | custom fusion | flops 589824 | bytes 6292736 | tf_op jit(solution)/shard_map/scatter-add | solution.py:142
  351.0 17.7 %fusion.35 = (bf16[192,8192]{0,1:T(8,128)(2,1)}, f32[192,8192]{0,1:T(8,128)}, f32[192,8192]{0,1:T(8,128)}) fusion(bf16[192,8192]{0,1:T(8,128)(2,1)} %copy.50, pred[8192]{0:T(1024)(128)(4,1)S(1)} %slice_compare_fusion, f32[192,8192]{0,1:T(8,128)} %copy.51, f32[192,8193]{0,1:T(8,128)} %scatter_custom_fusion.3, f32[192,8192]{0,1:T(8,128)} %copy.61), kind=kLoop, calls=%fused_computation.56 | loop fusion | flops 25165824 | bytes 37756928 | tf_op jit(solution)/shard_map/convert_element_type | solution.py:156
  368.7 6.0 %copy.63 = bf16[192,8192]{1,0:T(8,128)(2,1)} copy(bf16[192,8192]{0,1:T(8,128)(2,1)} %get-tuple-element.223) | data formatting | bytes 6291456
  374.7 8.7 %copy.64 = f32[192,8192]{1,0:T(8,128)} copy(f32[192,8192]{0,1:T(8,128)} %get-tuple-element.224) | data formatting | bytes 12582912
  383.4 8.7 %copy.65 = f32[192,8192]{1,0:T(8,128)} copy(f32[192,8192]{0,1:T(8,128)} %get-tuple-element.225) | data formatting | bytes 12582912
  (87 shorter events, 68.5 us)
Async XLA Ops:
  7.2 1.5 copy-start
  7.2 30.9 %copy-start.2 = (s32[8192]{0:T(1024)S(1)}, s32[8192]{0:T(1024)}, u32[]{:S(2)}) copy-start(s32[8192]{0:T(1024)} %param.15) | copy-start | bytes 98308
  7.2 116.4 %all-gather.2.cloned.1.call-start = ((), (), s32[]{:S(2)}) async-start(), calls=%async_computation.4 | async-start | bytes 7864320 | tf_op jit(solution)/shard_map/all_gather | solution.py:103
  38.1 20.7 %copy-start.3 = (bf16[192,8192]{1,0:T(8,128)(2,1)S(1)}, bf16[192,8192]{1,0:T(8,128)(2,1)}, u32[]{:S(2)}) copy-start(bf16[192,8192]{1,0:T(8,128)(2,1)} %param.14) | copy-start | bytes 9437188
  56.2 20.7 %all-to-all-start.1 = ((s32[1,32,96]{2,0,1:T(1,128)}), s32[1,32,96]{2,0,1:T(1,128)S(1)}, u32[]{:S(2)}, u32[]{:S(2)}) async-start(s32[1,32,96]{2,0,1:T(1,128)} %broadcast_in_dim.86), calls=%async_computation.1 | async-start | bytes 32768 | tf_op jit(solution)/shard_map/all_to_all | solution.py:91
  62.7 20.1 %copy-start.5 = (s32[6,4096]{1,0:T(8,128)S(1)}, s32[6,4096]{1,0:T(8,128)}, u32[]{:S(2)}) copy-start(s32[6,4096]{1,0:T(8,128)} %param.11) | copy-start | bytes 294916
  76.9 43.6 %all-to-all-start.2 = ((bf16[192,32,96]{2,0,1:T(8,128)(2,1)}), bf16[192,32,96]{2,0,1:T(8,128)(2,1)S(1)}, u32[]{:S(2)}, u32[]{:S(2)}) async-start(bf16[192,32,96]{2,0,1:T(8,128)(2,1)} %bitcast.13), calls=%async_computation.2 | async-start | bytes 3145728 | tf_op jit(solution)/shard_map/all_to_all | solution.py:88
  121.7 1.9 copy-start.4
  241.0 76.7 %all-to-all-start.3 = ((f32[192,32,96]{2,0,1:T(8,128)}), f32[192,32,96]{2,0,1:T(8,128)S(1)}, u32[]{:S(2)}, u32[]{:S(2)}) async-start(f32[192,32,96]{2,0,1:T(8,128)} %bitcast.65), calls=%async_computation.3 | async-start | bytes 6291456 | tf_op jit(solution)/shard_map/all_to_all | solution.py:132
  374.7 17.4 %copy-start.1 = (s32[65536]{0:T(1024)S(1)}, s32[65536]{0:T(1024)}, u32[]{:S(2)}) copy-start(s32[65536]{0:T(1024)} %param.13) | copy-start | bytes 786436
Sparse Core Ops, SparseCore 0:
  9.6 49.2 all-gather.1
where the time goes:
time: 402 us; the launch traced here: 400 us
  local copies, waits for them, and re-layouts  127 us (32%)
  other arithmetic  65.8 us (16%)
  waiting for transfers between devices  63.3 us (16%)
  blocking collectives  53.1 us (13%)
  matrix products  50 us (12%)
  between operations  21.3 us (5%)
  starting transfers between devices  13.6 us (3%)
  loops' own time  5.56 us (1%)
    unnamed x18, local copies, waits for them, and re-layouts  44.2 us
    psum x1, blocking collectives, body(): positives = lax.psum(fresh_total, ('clu', 'sub'))  38.8 us
    all_to_all x1, waiting for transfers between devices, body(): lax.all_to_all(buffer.reshape(col_width, clu_count * sub_count, slot_cap)...  32.3 us
    all_to_all x1, waiting for transfers between devices, body(): lax.all_to_all(label_table[:, picked], ('clu', 'sub'), split_axis=1, conc...  30.4 us
    dot_general x8, matrix products, one_block(): lax.dot_general(q_block, full_cols, (((1,), (0,)), ((), ())), preferred_e...  25.7 us
    dot_general x8, matrix products, one_block(): lax.dot_general(q_block, slopes, (((0,), (0,)), ((), ())), preferred_elem...  24.3 us
    scatter-add x1, other arithmetic, body(): summed = jnp.zeros((col_width, lab_rows + 1), jnp.float32).at[:, owner_re...  24 us
    scatter-add x1, other arithmetic, body(): jax.ops.segment_sum(jnp.ones(owner_requests.shape, jnp.float32), owner_re...  20.7 us
  transfers between devices with their start and end apart: 4, of which 2 were waited for; matrix products, arithmetic and copies ran while one was open for 24% of the time, Pallas kernels for 0%

commit v1 on v0

v1 whole, which is shorter than its diff:
```python
import math

import jax
import jax.numpy as jnp
from jax import lax
from jax.experimental import pallas as pl
from jax.sharding import PartitionSpec as P

LOSS_SCALE = 1048576


FOCUS_ALPHA = 0.25
BETA_FIRST = 0.9
BETA_SECOND = 0.999
LEARN_RATE = 0.01
EPSILON = 1e-08


def focal_terms(logits, target, weight):
    probability = jax.nn.sigmoid(logits)
    complement = 1.0 - probability
    soft_neg = jax.nn.softplus(-logits)
    soft_pos = jax.nn.softplus(logits)
    weight_row = weight[None, :]
    losses = weight_row * (
        target * FOCUS_ALPHA * complement * complement * soft_neg
        + (1.0 - target) * (1.0 - FOCUS_ALPHA) * probability * probability * soft_pos
    )
    slopes = weight_row * (
        target
        * -FOCUS_ALPHA
        * complement
        * complement
        * (2.0 * probability * soft_neg + complement)
        + (1.0 - target)
        * (1.0 - FOCUS_ALPHA)
        * probability
        * probability
        * (2.0 * complement * soft_pos + probability)
    )
    return (losses, slopes.astype(jnp.bfloat16))


def positive_mask(listed, columns):
    found = jnp.zeros((listed.shape[1], columns.shape[0]), jnp.float32)
    for k in range(listed.shape[0]):
        found = jnp.maximum(found, (listed[k][:, None] == columns[None, :]).astype(jnp.float32))
    return found


def adam_kernel(table_ref, first_ref, second_ref, rows_ref, table_out, first_out, second_out):
    col_width = table_ref.shape[0]
    flipped = jnp.transpose(rows_ref[...], (1, 0))
    grad = flipped[:col_width, :]
    hits = flipped[col_width : col_width + 1, :] > 0.5
    first = first_ref[...]
    second = second_ref[...]
    new_first = jnp.where(hits, BETA_FIRST * first + (1.0 - BETA_FIRST) * grad, first)
    new_second = jnp.where(
        hits, BETA_SECOND * second + (1.0 - BETA_SECOND) * grad * grad, second
    )
    base_table = table_ref[...].astype(jnp.float32)
    moved = base_table - LEARN_RATE * new_first / (jnp.sqrt(new_second) + EPSILON)
    table_out[...] = jnp.where(hits, moved, base_table).astype(jnp.bfloat16)
    first_out[...] = new_first
    second_out[...] = new_second


def adam_update(label_table, first_moment, second_moment, summed_rows):
    col_width, lab_rows = label_table.shape
    pad_width = summed_rows.shape[1]
    tile = 512
    spec = pl.BlockSpec((col_width, tile), lambda j: (0, j))
    return pl.pallas_call(
        adam_kernel,
        grid=(lab_rows // tile,),
        in_specs=[spec, spec, spec, pl.BlockSpec((tile, pad_width), lambda j: (j, 0))],
        out_specs=[spec, spec, spec],
        out_shape=[
            jax.ShapeDtypeStruct(label_table.shape, jnp.bfloat16),
            jax.ShapeDtypeStruct(first_moment.shape, jnp.float32),
            jax.ShapeDtypeStruct(second_moment.shape, jnp.float32),
        ],
    )(label_table, first_moment, second_moment, summed_rows)


def body(
    queries, pos_cols, label_ids, slot_of, label_table, label_freq, first_moment, second_moment
):
    clu_count = lax.axis_size("clu")
    sub_count = lax.axis_size("sub")
    my_sub = lax.axis_index("sub")
    n_dev = clu_count * sub_count
    list_len = label_ids.shape[0]
    col_width = label_table.shape[0]
    lab_rows = label_table.shape[1]
    width = col_width * sub_count
    slot_cap = 3 * list_len // clu_count
    inv_root = 1.0 / math.sqrt(width)
    axes = ("clu", "sub")

    slot_ids = slot_of[label_ids]
    owner_of = slot_ids // lab_rows
    local_row = slot_ids % lab_rows
    one_hot = (owner_of[:, None] == jnp.arange(clu_count, dtype=jnp.int32)[None, :]).astype(
        jnp.int32
    )
    slot_rank = jnp.sum(jnp.cumsum(one_hot, axis=0) * one_hot, axis=1) - 1
    key = owner_of * slot_cap + slot_rank
    match = key[:, None] == jnp.arange(clu_count * slot_cap, dtype=jnp.int32)[None, :]
    requests = jnp.max(jnp.where(match, local_row[:, None], -1), axis=0)
    requests = jnp.where(requests < 0, lab_rows, requests)
    inverse = jnp.max(jnp.where(match, jnp.arange(list_len, dtype=jnp.int32)[:, None], -1), axis=0)
    inverse = jnp.where(inverse < 0, list_len, inverse)

    columns = my_sub * list_len + jnp.arange(list_len, dtype=jnp.int32)
    lower = my_sub * list_len
    fresh_total = jnp.zeros((), jnp.int32)
    for k in range(pos_cols.shape[0]):
        fresh = jnp.logical_and(pos_cols[k] >= lower, pos_cols[k] < lower + list_len)
        for j in range(k):
            fresh = jnp.logical_and(fresh, pos_cols[j] != pos_cols[k])
        fresh_total = fresh_total + jnp.sum(fresh.astype(jnp.int32))

    wanted = jnp.broadcast_to(
        requests.reshape(clu_count, 1, slot_cap), (clu_count, sub_count, slot_cap)
    ).reshape(n_dev, slot_cap)
    wanted = jnp.concatenate(
        [wanted, jnp.broadcast_to(fresh_total, (n_dev, 1)).astype(jnp.int32)], axis=1
    )
    asked_all = lax.all_to_all(wanted, axes, split_axis=0, concat_axis=0, tiled=True)
    positives = jnp.sum(asked_all[:, slot_cap]).astype(jnp.float32)
    asked = asked_all[:, :slot_cap]
    factor = LOSS_SCALE / (math.sqrt(width) * positives)

    picked = jnp.clip(asked, 0, lab_rows - 1).reshape(-1)
    table_rows = label_table.T
    sent_rows = table_rows[picked].reshape(n_dev, slot_cap, col_width)
    got = lax.all_to_all(sent_rows, axes, split_axis=0, concat_axis=0, tiled=True)
    got = got.reshape(clu_count, sub_count, slot_cap, col_width)
    fetched = got[owner_of, :, slot_rank, :].reshape(list_len, width)

    all_freq = lax.all_gather(label_freq, "clu", axis=0, tiled=True)
    fetched_freq = all_freq[slot_ids]
    weights = 1.0 / (1.0 + jnp.log1p(fetched_freq.astype(jnp.float32)))

    initial = (jnp.zeros((list_len, width), jnp.float32), jnp.zeros((), jnp.float32))
    arrived = lax.all_gather(queries, "sub", axis=0, tiled=True)
    count_rows = arrived.shape[0]
    block = 512

    def one_block(step, partial_value):
        q_block = lax.dynamic_slice_in_dim(arrived, step * block, block, 0)
        p_block = lax.dynamic_slice_in_dim(pos_cols, step * block, block, 1)
        target = positive_mask(p_block, columns)
        logits = (
            lax.dot_general(
                q_block, fetched, (((1,), (1,)), ((), ())), preferred_element_type=jnp.float32
            )
            * inv_root
        )
        losses, slopes = focal_terms(logits, target, weights)
        gradient = partial_value[0] + lax.dot_general(
            slopes, q_block, (((0,), (0,)), ((), ())), preferred_element_type=jnp.float32
        )
        return (gradient, partial_value[1] + jnp.sum(losses))

    gradient, loss_here = lax.fori_loop(0, count_rows // block, one_block, initial)
    outgoing = gradient * factor
    padded = jnp.concatenate([outgoing, jnp.zeros((1, width), jnp.float32)], axis=0)
    buffer = padded[inverse].reshape(clu_count, slot_cap, sub_count, col_width)
    buffer = jnp.transpose(buffer, (0, 2, 1, 3)).reshape(n_dev, slot_cap, col_width)
    loss_row = jnp.zeros((n_dev, 1, col_width), jnp.float32).at[:, 0, 0].set(loss_here)
    buffer = jnp.concatenate([buffer, loss_row], axis=1)
    received = lax.all_to_all(buffer, axes, split_axis=0, concat_axis=0, tiled=True)
    loss_sum = jnp.sum(received[:, slot_cap, 0])
    incoming = received[:, :slot_cap, :].reshape(n_dev * slot_cap, col_width)
    pad_width = 256 * ((col_width + 1 + 255) // 256)
    incoming = jnp.concatenate(
        [
            incoming,
            jnp.ones((n_dev * slot_cap, 1), jnp.float32),
            jnp.zeros((n_dev * slot_cap, pad_width - col_width - 1), jnp.float32),
        ],
        axis=1,
    )
    owner_requests = asked.reshape(-1)
    summed_rows = (
        jnp.zeros((lab_rows + 1, pad_width), jnp.float32).at[owner_requests].add(incoming)
    )
    new_table, new_first, new_second = adam_update(
        label_table, first_moment, second_moment, summed_rows
    )
    mean_loss = loss_sum / positives
    return (new_table, new_first, new_second, mean_loss)


def solution(mesh):
    in_specs = (
        P(("clu", "sub"), None),
        P(None, "clu"),
        P(("clu", "sub")),
        P(),
        P("sub", "clu"),
        P("clu"),
        P("sub", "clu"),
        P("sub", "clu"),
    )
    out_specs = (P("sub", "clu"), P("sub", "clu"), P("sub", "clu"), P())
    return jax.shard_map(body, mesh=mesh, in_specs=in_specs, out_specs=out_specs, check_vma=False)
```

time: 402 us -> 329 us (0.82)
  local copies, waits for them, and re-layouts: 127 us -> 52 us
  other arithmetic: 65.8 us -> 32.7 us
  Pallas kernels: 0 us -> 20.5 us
  waiting for transfers between devices: 63.3 us -> 72.9 us
  blocking collectives: 53.1 us -> 58 us
    all_gather x0 -> x1, blocking collectives: none -> 58 us  [body(): all_freq = lax.all_gather(label_freq, 'clu', axis=0, tiled=True)]
    psum x1 -> x0, blocking collectives: 38.8 us -> none  [body(): positives = lax.psum(fresh_total, ('clu', 'sub'))]
    unnamed x18 -> x8, local copies, waits for them, and re-layouts: 44.2 us -> 6.07 us
    scatter x3 -> x2, local copies, waits for them, and re-layouts: 30.9 us -> 0.42 us  [body(): jnp.zeros((n_dev, 1, col_width), jnp.float32).at[:, 0, 0].set(loss_here)]
    pallas_call x0 -> x1, Pallas kernels: none -> 20.5 us  [adam_update(): pl.pallas_call(adam_kernel, grid=(lab_rows // tile,), in_specs=[spec, spe...]
    scatter-add x2 -> x1, other arithmetic: 44.8 us -> 24.3 us  [body(): jnp.zeros((lab_rows + 1, pad_width), jnp.float32).at[owner_requests]]
    convert_element_type x1 -> x0, other arithmetic: 17.7 us -> none  [body(): new_table = jnp.where(hits, moved, base_table).astype(jnp.bfloat16)]
    all_to_all x1 -> x0, blocking collectives: 14.3 us -> none  [body(): lax.all_to_all(wanted, ('clu', 'sub'), split_axis=0, concat_axis=0, tiled...]
  transfers between devices with their start and end apart: 4 -> 4, of which waited for: 2 -> 2; matrix products, arithmetic and copies ran while one was open for 24% -> 11% of each run, Pallas kernels for 0% -> 0%
where the time goes in v1:
time: 329 us; the launch traced here: 327 us
  waiting for transfers between devices  72.9 us (22%)
  blocking collectives  58 us (18%)
  local copies, waits for them, and re-layouts  52 us (16%)
  matrix products  49.4 us (15%)
  other arithmetic  32.7 us (10%)
  Pallas kernels  20.5 us (6%)
  between operations  20.5 us (6%)
  starting transfers between devices  15.7 us (5%)
  loops' own time  5.58 us (2%)
    all_to_all x1, waiting for transfers between devices, body(): lax.all_to_all(buffer, axes, split_axis=0, concat_axis=0, tiled=True)  71 us
    all_gather x1, blocking collectives, body(): all_freq = lax.all_gather(label_freq, 'clu', axis=0, tiled=True)  58 us
    dot_general x8, matrix products, one_block(): lax.dot_general(q_block, fetched, (((1,), (1,)), ((), ())), preferred_ele...  26.1 us
    scatter-add x1, other arithmetic, body(): jnp.zeros((lab_rows + 1, pad_width), jnp.float32).at[owner_requests]  24.3 us
    dot_general x8, matrix products, one_block(): lax.dot_general(slopes, q_block, (((0,), (0,)), ((), ())), preferred_elem...  23.3 us
    pallas_call x1, Pallas kernels, adam_update(): pl.pallas_call(adam_kernel, grid=(lab_rows // tile,), in_specs=[spec, spe...  20.5 us
    gather x1, local copies, waits for them, and re-layouts, body(): sent_rows = table_rows[picked].reshape(n_dev, slot_cap, col_width)  15 us
    slice x8, local copies, waits for them, and re-layouts, positive_mask(): listed[k][:, None] == columns[None, :]  8.32 us
  transfers between devices with their start and end apart: 4, of which 2 were waited for; matrix products, arithmetic and copies ran while one was open for 11% of the time, Pallas kernels for 0%

profile of v1, /device:TPU:0, one launch (start us, length us, event | category | flops | bytes accessed | tf_op | source)
XLA Modules:
  0.0 327.4 jit_solution(7527410590156932840)
XLA Ops:
  18.7 7.3 %all-to-all-start = ((s32[32,1,97]{2,1,0:T(1,128)}), s32[32,1,97]{2,1,0:T(1,128)S(1)}, u32[]{:S(2)}, u32[]{:S(2)}) async-start(s32[32,1,97]{2,1,0:T(1,128)} %bitcast.4), calls=%async_computation | async-start | bytes 32768 | tf_op jit(solution)/shard_map/all_to_all | solution.py:131
  26.0 5.9 %copy.29 = bf16[192,8192]{0,1:T(8,128)(2,1)} copy(bf16[192,8192]{1,0:T(8,128)(2,1)} %table_ref.1) | data formatting | bytes 6291456 | tf_op args[4]
  33.2 15.0 %gather_fusion.2 = bf16[3072,192]{1,0:T(8,128)(2,1)} fusion(bf16[8192,192]{1,0:T(8,128)(2,1)} %bitcast.55, s32[3072]{0:T(1024)S(1)} %broadcast_clamp_fusion.1), kind=kCustom, calls=%fused_computation.2 | custom fusion | bytes 2371584 | tf_op jit(solution)/shard_map/gather | solution.py:138
  48.2 4.7 %all-to-all-start.1 = ((bf16[32,96,192]{2,1,0:T(8,128)(2,1)}), bf16[32,96,192]{2,1,0:T(8,128)(2,1)S(1)}, u32[]{:S(2)}, u32[]{:S(2)}) async-start(bf16[32,96,192]{2,1,0:T(8,128)(2,1)} %bitcast.62), calls=%async_computation.1 | async-start | bytes 3145728 | tf_op jit(solution)/shard_map/all_to_all | solution.py:139
  52.9 58.0 %all_gather.6 = s32[65536]{0:T(1024)S(1)} all-gather(s32[8192]{0:T(1024)S(1)} %copy-done.2), channel_id=1, replica_groups=mesh['clu'=8,'sub'=4] {'clu'}, dimensions={0}, use_global_device_ids=true | all-gather | bytes 294912 | tf_op jit(solution)/shard_map/all_gather | solution.py:143
  116.4 2.9 gather_fusion.3
  119.9 63.3 %while.17 = (s32[]{:T(128)}, f32[256,768]{1,0:T(8,128)S(1)}, f32[]{:T(128)}, f32[256]{0:T(256)S(1)}, s32[6,4096]{1,0:T(8,128)}, /*index=5*/bf16[4096,768]{1,0:T(...) while((s32[]{:T(128)}, f32[256,768]{1,0:T(8,128)S(1)}, ...), condition=%wide.region_12.13_spmd.clone, body=%wide.region_10.12_spmd.clone.sunk | while | flops 416022784 | bytes 4642125 | solution.py:168
  120.9 3.3 fusion.61
  128.8 3.3 fusion.61
  132.8 2.9 convolution_add_fusion.2
  136.8 3.3 fusion.61
  144.7 3.3 fusion.61
  152.6 3.3 fusion.61
  156.5 2.9 convolution_add_fusion.2
  160.5 3.3 fusion.61
  168.4 3.3 fusion.61
  176.3 3.3 fusion.61
  180.2 2.9 convolution_add_fusion.2
  185.9 3.5 %reshape.349 = f32[8,96,4,192]{3,2,1,0:T(4,128)} reshape(f32[768,768]{1,0:T(8,128)S(1)} %gather_fusion.4) | data formatting | bytes 4718592 | tf_op jit(solution)/shard_map/reshape | solution.py:171
  189.4 3.3 %copy.33 = f32[8,4,96,192]{2,3,1,0:T(8,128)S(1)} copy(f32[8,4,96,192]{3,1,2,0:T(4,128)} %bitcast.60) | data formatting | bytes 4718592 | tf_op jit(solution)/shard_map/transpose | solution.py:172
  195.7 3.7 %all-to-all-start.2 = ((f32[32,97,192]{1,2,0:T(8,128)}), f32[32,97,192]{1,2,0:T(8,128)S(1)}, u32[]{:S(2)}, u32[]{:S(2)}) async-start(f32[32,97,192]{1,2,0:T(8,128)} %pad_maximum_fusion), calls=%async_computation.2 | async-start | bytes 6291456 | tf_op jit(solution)/shard_map/all_to_all | solution.py:175
  199.6 71.0 %all-to-all-done.2 = f32[32,97,192]{1,2,0:T(8,128)S(1)} async-done(((f32[32,97,192]{1,2,0:T(8,128)}), f32[32,97,192]{1,2,0:T(8,128)S(1)}, u32[]{:S(2)}, u32[]{:S(2)}) %all-to-all-start.2) | async-done | bytes 2383904 | tf_op jit(solution)/shard_map/all_to_all | solution.py:175
  274.6 24.3 %scatter_custom_fusion.rows_ref = f32[8193,256]{1,0:T(8,128)} fusion(s32[3072]{0:T(1024)S(1)} %bitcast.81, f32[]{:T(128)} %constant.158.clone.1, f32[3072,192]{1,0:T(8,128)} %bitcast.58, f32[]{:T(128)} %constant.198, f32[256]{0:T(256)S(1)} %pad.8.clone, f32[256]{0:T(256)S(1)} %pad.7.clone), kind=kCustom, calls=%fused_computation.49 | custom fusion | flops 2359296 | bytes 10750984 | tf_op jit(solution)/shard_map/scatter-add | solution.py:189
  298.9 20.5 %shard_map.111 = (bf16[192,8192]{1,0:T(8,128)(2,1)}, f32[192,8192]{1,0:T(8,128)}, f32[192,8192]{1,0:T(8,128)}) custom-call(bf16[192,8192]{1,0:T(8,128)(2,1)} %table_ref.1, f32[192,8192]{1,0:T(8,128)} %first_ref.1, f32[192,8192]{1,0:T(8,128)} %second_ref.1, f32[8193,256]{1,0:T(8,128)} %scatter_custom_fusion.rows_ref), custom_call_target="tpu_custom_call" | custom-call | tf_op jit(solution)/shard_map/pallas_call | solution.py:74
  (78 shorter events, 46.4 us)
Async XLA Ops:
  7.2 1.4 copy-start
  7.2 112.7 %all-gather.2.cloned.1.call-start = ((), (), s32[]{:S(2)}) async-start(), calls=%async_computation.3 | async-start | bytes 7864320 | tf_op jit(solution)/shard_map/all_gather | solution.py:148
  18.7 14.4 %all-to-all-start = ((s32[32,1,97]{2,1,0:T(1,128)}), s32[32,1,97]{2,1,0:T(1,128)S(1)}, u32[]{:S(2)}, u32[]{:S(2)}) async-start(s32[32,1,97]{2,1,0:T(1,128)} %bitcast.4), calls=%async_computation | async-start | bytes 32768 | tf_op jit(solution)/shard_map/all_to_all | solution.py:131
  48.2 4.7 %copy-start.2 = (s32[8192]{0:T(1024)S(1)}, s32[8192]{0:T(1024)}, u32[]{:S(2)}) copy-start(s32[8192]{0:T(1024)} %param.17) | copy-start | bytes 98308
  48.2 65.8 %all-to-all-start.1 = ((bf16[32,96,192]{2,1,0:T(8,128)(2,1)}), bf16[32,96,192]{2,1,0:T(8,128)(2,1)S(1)}, u32[]{:S(2)}, u32[]{:S(2)}) async-start(bf16[32,96,192]{2,1,0:T(8,128)(2,1)} %bitcast.62), calls=%async_computation.1 | async-start | bytes 3145728 | tf_op jit(solution)/shard_map/all_to_all | solution.py:139
  195.7 75.0 %all-to-all-start.2 = ((f32[32,97,192]{1,2,0:T(8,128)}), f32[32,97,192]{1,2,0:T(8,128)S(1)}, u32[]{:S(2)}, u32[]{:S(2)}) async-start(f32[32,97,192]{1,2,0:T(8,128)} %pad_maximum_fusion), calls=%async_computation.2 | async-start | bytes 6291456 | tf_op jit(solution)/shard_map/all_to_all | solution.py:175
  298.9 20.5 %copy-start.1 = (s32[65536]{0:T(1024)S(1)}, s32[65536]{0:T(1024)}, u32[]{:S(2)}) copy-start(s32[65536]{0:T(1024)} %param.15) | copy-start | bytes 786436
Sparse Core Ops, SparseCore 0:
  9.6 50.7 all-gather.1
